TPU v7x, 32 devices: a whole 2x2x4 slice. The times are simulated.
32 devices in a mesh: fsdp: 8 (over z, y), rows: 4 (over x, core).
Axes of the slice: x: 2, y: 2, z: 4, core: 2. Of those that a mesh axis runs over, the one named last changes fastest.
Arguments:
- frames: bfloat16 [8, 12, 16, 1536], P('fsdp', 'rows'), may hold values from -6 to 6
- kernel: float32 [7, 7, 1536], replicated, may hold values from -0.875 to 0.875
- kernel_bias: float32 [1536], replicated, may hold values from -3 to 3
- layer_norm_weight: float32 [1536], replicated, may hold values from 0.25 to 1.75
- layer_norm_bias: float32 [1536], replicated, may hold values from -3 to 3
- up_weight: bfloat16 [1536, 6144], P('fsdp', 'rows'), may hold values from -1 to 1, as said below
- up_bias: float32 [6144], P('rows'), may hold values from -3 to 3
- grn_gamma: float32 [6144], P('rows'), may hold values from 0.2 to 1
- grn_beta: float32 [6144], P('rows'), may hold values from -3 to 3
- grad_out: bfloat16 [8, 12, 16, 6144], P('fsdp', None, None, 'rows'), may hold values from -8 to 8, as said below
Outputs:
- activation: bfloat16 [8, 12, 16, 6144], P('fsdp', None, None, 'rows')
- frames_grad: bfloat16 [8, 12, 16, 1536], P('fsdp', 'rows')
- up_weight_grad: float32 [1536, 6144], P('fsdp', 'rows')
- kernel_grad: float32 [7, 7, 1536], replicated
Inputs may be any that keep to these rules, and one draw needn't show every extreme that they name: `up_weight`: entries lie within the bounds. `grad_out`: entries lie within the bounds.
All inputs are finite; a program needn't handle non-finite values.
Results may differ from a plain program's by a relative error of at most 0.014.
Values may be sent and summed in bfloat16 or wider, within the bound.
No kernel may reach another device: no remote copies, remote signals or barrier semaphores. Data moves between devices by JAX's collectives and lax.ppermute only.
A program may use at most 64 MiB of HBM per device.

v0:
```python
import functools
import jax
import jax.numpy as jnp
from jax import lax
from jax.sharding import PartitionSpec as P

FF = 6144


def extended(block, sides, width):
    for axis, dim in sides:
        count = lax.axis_size(axis)
        forward = [(i, i + 1) for i in range(count - 1)]
        backward = [(target, source) for source, target in forward]
        low = lax.ppermute(
            lax.slice_in_dim(block, block.shape[dim] - width, None, axis=dim), axis, forward
        )
        high = lax.ppermute(lax.slice_in_dim(block, 0, width, axis=dim), axis, backward)
        block = jnp.concatenate([low, block, high], axis=dim)
    return block


def _bit_steps(axes):
    steps = []
    for axis in axes:
        size = lax.axis_size(axis)
        assert size & size - 1 == 0
        mask = 1
        while mask < size:
            steps.append((axis, mask, size))
            mask *= 2
    return steps


def tree_allreduce(value, axes):
    shape = value.shape
    flat = value.reshape(-1)
    steps = _bit_steps(axes)
    assert flat.shape[0] % (1 << len(steps)) == 0
    bits = []
    for axis, mask, size in steps:
        bit = lax.axis_index(axis) // mask % 2
        bits.append(bit)
        halves = flat.reshape(2, -1)
        keep = lax.dynamic_index_in_dim(halves, bit, keepdims=False)
        give = lax.dynamic_index_in_dim(halves, 1 - bit, keepdims=False)
        perm = [(j, j ^ mask) for j in range(size)]
        flat = keep + lax.ppermute(give, axis, perm)
    for (axis, mask, size), bit in reversed(list(zip(steps, bits))):
        perm = [(j, j ^ mask) for j in range(size)]
        other = lax.ppermute(flat, axis, perm)
        flat = jnp.where(bit == 0, jnp.concatenate([flat, other]), jnp.concatenate([other, flat]))
    return flat.reshape(shape)


def tree_reduce_scatter(chunks, axis):
    size = lax.axis_size(axis)
    assert chunks.shape[0] == size and size & size - 1 == 0
    me = lax.axis_index(axis)
    data = chunks
    mask = 1
    while mask < size:
        bit = me // mask % 2
        pairs = data.reshape((data.shape[0] // 2, 2) + data.shape[1:])
        keep = lax.dynamic_index_in_dim(pairs, bit, axis=1, keepdims=False)
        give = lax.dynamic_index_in_dim(pairs, 1 - bit, axis=1, keepdims=False)
        perm = [(j, j ^ mask) for j in range(size)]
        data = keep.astype(jnp.float32) + lax.ppermute(give, axis, perm).astype(jnp.float32)
        mask *= 2
    return data[0]


def fsdp_ring(mesh):
    count = mesh.shape["fsdp"]
    try:
        members = [mesh.devices[j, 0] for j in range(count)]
        spots = [(d.coords[2], d.coords[1]) for d in members]
        zs = sorted({z for z, _ in spots})
        ys = sorted({y for _, y in spots})
        rows_a, cols_b = (len(zs), len(ys))
        where = {(zs.index(z), ys.index(y)): j for j, (z, y) in enumerate(spots)}
        assert len(where) == count == rows_a * cols_b and rows_a % 2 == 0 and (cols_b >= 2)
        cells = [(a, 0) for a in range(rows_a)]
        for k, a in enumerate(range(rows_a - 1, -1, -1)):
            span = range(1, cols_b) if k % 2 == 0 else range(cols_b - 1, 0, -1)
            cells += [(a, b) for b in span]
        ring = [where[c] for c in cells]
        assert sorted(ring) == list(range(count))
    except Exception:
        ring = list(range(count))
    return ring


def ring_all_gather(block, axis, ring, held=None):
    count = len(ring)
    place = [0] * count
    for k, j in enumerate(ring):
        place[j] = k
    ring_arr = jnp.array(ring, jnp.int32)
    me = lax.axis_index(axis)
    spot = jnp.array(place, jnp.int32)[me]
    forward = [(ring[k], ring[(k + 1) % count]) for k in range(count)]
    backward = [(ring[k], ring[(k - 1) % count]) for k in range(count)]
    ahead = count // 2
    behind = count - 1 - ahead
    gathered = jnp.zeros((count,) + block.shape, block.dtype)
    gathered = lax.dynamic_update_index_in_dim(gathered, block, me, 0)
    cw = block
    ccw = block
    for s in range(1, ahead + 1):
        cw = lax.ppermute(cw, axis, forward)
        if s <= behind:
            ccw = lax.ppermute(ccw, axis, backward)
        if s == 1 and held is not None:
            cw, ccw, held = lax.optimization_barrier((cw, ccw, held))
        gathered = lax.dynamic_update_index_in_dim(gathered, cw, ring_arr[(spot - s) % count], 0)
        if s <= behind:
            gathered = lax.dynamic_update_index_in_dim(
                gathered, ccw, ring_arr[(spot + s) % count], 0
            )
    return (gathered.reshape((count * block.shape[0],) + block.shape[1:]), held)


def ring_reduce_scatter(terms, axis, ring):
    count = len(ring)
    place = [0] * count
    for k, j in enumerate(ring):
        place[j] = k
    ring_arr = jnp.array(ring, jnp.int32)
    me = lax.axis_index(axis)
    spot = jnp.array(place, jnp.int32)[me]
    forward = [(ring[k], ring[(k + 1) % count]) for k in range(count)]
    backward = [(ring[k], ring[(k - 1) % count]) for k in range(count)]
    ahead = count // 2
    behind = count - 1 - ahead

    def term(offset):
        return lax.dynamic_index_in_dim(terms, ring_arr[(spot + offset) % count], 0, keepdims=False)

    total = term(0).astype(jnp.float32)
    cw = term(ahead)
    ccw = term(-behind) if behind else None
    for s in range(1, ahead + 1):
        cw = lax.ppermute(cw, axis, forward)
        if s <= behind:
            ccw = lax.ppermute(ccw, axis, backward)
        if s < ahead:
            cw = (cw.astype(jnp.float32) + term(ahead - s).astype(jnp.float32)).astype(terms.dtype)
        else:
            total = total + cw.astype(jnp.float32)
        if s < behind:
            ccw = (ccw.astype(jnp.float32) + term(s - behind).astype(jnp.float32)).astype(
                terms.dtype
            )
        elif s == behind:
            total = total + ccw.astype(jnp.float32)
    return total


def tree_all_gather(block, axis):
    size = lax.axis_size(axis)
    assert size & size - 1 == 0
    me = lax.axis_index(axis)
    data = block[None]
    mask = 1
    while mask < size:
        bit = me // mask % 2
        perm = [(j, j ^ mask) for j in range(size)]
        other = lax.ppermute(data, axis, perm)
        data = jnp.where(bit == 0, jnp.concatenate([data, other]), jnp.concatenate([other, data]))
        mask *= 2
    return data.reshape((size * block.shape[0],) + block.shape[1:])


def conv_rows(framed, kern, kbias):
    rows = framed.shape[0] - 6
    cols = framed.shape[1]
    wide = jnp.pad(framed, ((0, 0), (3, 3), (0, 0)))
    total = jnp.zeros((rows, cols, framed.shape[2]), jnp.float32) + kbias
    for i in range(kern.shape[0]):
        for j in range(kern.shape[1]):
            total = total + wide[i : i + rows, j : j + cols].astype(jnp.float32) * kern[i, j]
    return total


def back_conv(grad_pad, kern):
    rows = grad_pad.shape[0] - 6
    cols = grad_pad.shape[1]
    wide = jnp.pad(grad_pad, ((0, 0), (3, 3), (0, 0)))
    total = jnp.zeros((rows, cols, grad_pad.shape[2]), jnp.float32)
    for i in range(kern.shape[0]):
        for j in range(kern.shape[1]):
            total = (
                total
                + wide[6 - i : 6 - i + rows, 6 - j : 6 - j + cols].astype(jnp.float32) * kern[i, j]
            )
    return total


def kern_grad(framed, grad_rows):
    rows = grad_rows.shape[0]
    cols = grad_rows.shape[1]
    wide = jnp.pad(framed, ((0, 0), (3, 3), (0, 0)))
    grad_f = grad_rows.astype(jnp.float32)
    parts = []
    for i in range(7):
        for j in range(7):
            parts.append(
                jnp.sum(wide[i : i + rows, j : j + cols].astype(jnp.float32) * grad_f, axis=(0, 1))
            )
    return jnp.stack(parts).reshape(7, 7, grad_rows.shape[2])


def apply_layer_norm(activation_rows, scale_factor, offset_bias):
    centered_input = activation_rows - jnp.mean(activation_rows, axis=-1, keepdims=True)
    inverse_deviation = lax.rsqrt(
        jnp.mean(centered_input * centered_input, axis=-1, keepdims=True) + 1e-06
    )
    standardized_input = centered_input * inverse_deviation
    return (
        (standardized_input * scale_factor + offset_bias).astype(jnp.bfloat16),
        standardized_input,
        inverse_deviation,
    )


def gelu_grad(value):
    return (
        0.5 * (1.0 + jax.scipy.special.erf(value * 0.7071067811865476))
        + value * jnp.exp(-0.5 * value * value) * 0.3989422804014327
    )


def layer_norm_backward(normed_input_gradient, scale_factor, standardized_input, inverse_deviation):
    scaled_output = normed_input_gradient * scale_factor
    return (
        inverse_deviation
        * (
            scaled_output
            - jnp.mean(scaled_output, axis=-1, keepdims=True)
            - standardized_input
            * jnp.mean(scaled_output * standardized_input, axis=-1, keepdims=True)
        )
    ).astype(jnp.bfloat16)


def body(
    ring,
    frames,
    kernel,
    kernel_bias,
    layer_norm_weight,
    layer_norm_bias,
    up_weight,
    up_bias,
    grn_gamma,
    grn_beta,
    grad_out,
):
    slab = frames[0]
    chans = slab.shape[2]
    columns, slab = ring_all_gather(up_weight, "fsdp", ring, slab)
    padded = extended(slab, (("rows", 0),), 3)
    activation_rows = conv_rows(padded, kernel, kernel_bias)
    normed_output, standardized_input, inverse_deviation = apply_layer_norm(
        activation_rows, layer_norm_weight, layer_norm_bias
    )
    whole = tree_all_gather(normed_output, "rows")
    height = whole.shape[0]
    cols = whole.shape[1]
    flat = whole.reshape(-1, chans)
    pre = jnp.dot(flat, columns, preferred_element_type=jnp.float32) + up_bias
    post = jax.nn.gelu(pre, approximate=False)
    norms = jnp.sqrt(jnp.sum(post * post, axis=0) + 1e-06)
    cot_f = grad_out[0].reshape(flat.shape[0], -1).astype(jnp.float32)
    dnorm = grn_gamma * jnp.sum(cot_f * post, axis=0)
    norm_total = lax.psum(jnp.sum(norms), "rows")
    denom = norm_total / FF + 1e-06
    ratio = norms / denom
    output = (grn_gamma * (post * ratio) + grn_beta + post).astype(jnp.bfloat16)
    cross = lax.psum(jnp.sum(dnorm * norms), "rows")
    dnorms = dnorm / denom - cross / (denom * denom) / FF
    dpost = cot_f * (1.0 + grn_gamma * ratio) + post * (dnorms / norms)
    dpre = (dpost * gelu_grad(pre)).astype(jnp.bfloat16)
    w_term = lax.dot_general(
        flat, dpre, (((0,), (0,)), ((), ())), preferred_element_type=jnp.float32
    )
    n_fsdp = lax.axis_size("fsdp")
    up_grad = ring_reduce_scatter(
        w_term.astype(jnp.bfloat16).reshape((n_fsdp, chans // n_fsdp, -1)), "fsdp", ring
    )
    dpre_rows = dpre.reshape(height, cols, -1)
    group_terms = jnp.einsum(
        "hwf,cf->hwc", dpre_rows, columns, preferred_element_type=jnp.float32
    ).astype(jnp.bfloat16)
    n_rows = lax.axis_size("rows")
    normed_input_gradient = tree_reduce_scatter(
        group_terms.reshape((n_rows, height // n_rows) + group_terms.shape[1:]), "rows"
    )
    activation_gradient = layer_norm_backward(
        normed_input_gradient, layer_norm_weight, standardized_input, inverse_deviation
    )
    grad_pad = extended(activation_gradient, (("rows", 0),), 3)
    dframe = back_conv(grad_pad, kernel).astype(jnp.bfloat16)
    kernel_local = kern_grad(padded, activation_gradient)
    n_rows = lax.axis_size("rows")
    kernel_part = tree_reduce_scatter(kernel_local.reshape(n_rows, -1), "rows")
    kernel_total = tree_all_gather(lax.psum(kernel_part, "fsdp"), "rows").reshape(
        kernel_local.shape
    )
    activation = output.reshape(1, height, cols, -1)
    return (activation, dframe.reshape((1,) + dframe.shape), up_grad, kernel_total)


def solution(mesh):
    placed = (
        P("fsdp", "rows", None, None),
        P(),
        P(),
        P(),
        P(),
        P("fsdp", "rows"),
        P("rows"),
        P("rows"),
        P("rows"),
        P("fsdp", None, None, "rows"),
    )
    return jax.shard_map(
        functools.partial(body, fsdp_ring(mesh)),
        mesh=mesh,
        in_specs=placed,
        out_specs=(
            P("fsdp", None, None, "rows"),
            P("fsdp", "rows", None, None),
            P("fsdp", "rows"),
            P(),
        ),
        check_vma=False,
    )
```

profile of v0, /device:TPU:0, one launch (start us, length us, event | category | flops | bytes accessed | tf_op | source)
XLA Modules:
  0.0 275.6 jit_solution(5724363738028582769)
XLA Ops:
  7.2 3.1 %collective-permute-start = (bf16[192,1536]{1,0:T(8,128)(2,1)}, bf16[192,1536]{1,0:T(8,128)(2,1)S(1)}, u32[]{:S(2)}, u32[]{:S(2)}) collective-permute-start(bf16[192,1536]{1,0:T(8,128)(2,1)} %param.19), channel_id=1, source_target_pairs={{0,8},{8,16},{16,24},{24,28},{28,20},{20,12},{12,4},{4,0},{1,9},{9... | collective-permute-start | bytes 1769480 | tf_op jit(solution)/shard_map/ppermute | solution.py:111
  22.8 2.0 fusion.160
  33.7 1.7 slice_reduce_fusion.48
  35.4 1.8 slice_reduce_fusion.47
  48.1 1.9 collective-permute-start.6
  50.2 1.8 collective-permute-done.3
  52.5 3.4 %fusion.158 = (f32[3,16]{1,0:T(4,128)S(1)}, f32[3,16,1536]{2,1,0:T(8,128)S(1)}) fusion(f32[1536]{0:T(1024)S(1)} %get-tuple-element.105, bf16[9,22,1536]{2,1,0:T(8,128)(2,1)S(1)} %select_maximum_fusion.2, f32[1536]{0:T(1024)S(1)} %get-tuple-element.106, f32[1536]{0:T(1024)S(1)} %get-tuple-element.59, f32[1536]{0:T(1024)S(1)} %get-tuple-element.60, ...), kind=kLoop, calls=%fused_computation.380 | loop fusion | flops 10911696 | bytes 7827648 | tf_op jit(solution)/shard_map/reduce_sum | solution.py:215
  56.3 4.1 %collective-permute-start.4 = (bf16[1,3,16,1536]{3,2,1,0:T(8,128)(2,1)S(1)}, bf16[1,3,16,1536]{3,2,1,0:T(8,128)(2,1)S(1)}, u32[]{:S(2)}, u32[]{:S(2)}) collective-permute-start(bf16[1,3,16,1536]{3,2,1,0:T(8,128)(2,1)S(1)} %fusion.149), channel_id=1, source_target_pairs={{0,1},{1,0},{2,3},{3,2},{4,5},{5,4},{6,7},{7,6},{8,9},{9,8},{10,11... | collective-permute-start | bytes 442376 | tf_op jit(solution)/shard_map/ppermute | solution.py:169
  62.1 2.1 collective-permute-start.8
  64.6 6.1 %collective-permute-done.5 = bf16[2,3,16,1536]{3,2,1,0:T(8,128)(2,1)S(1)} collective-permute-done((bf16[2,3,16,1536]{3,2,1,0:T(8,128)(2,1)S(1)}, bf16[2,3,16,1536]{3,2,1,0:T(8,128)(2,1)S(1)}, u32[]{:S(2)}, u32[]{:S(2)}) %collective-permute-start.5) | collective-permute-done | bytes 294944 | tf_op jit(solution)/shard_map/ppermute | solution.py:169
  70.8 6.2 %collective-permute-done.8 = bf16[192,1536]{1,0:T(8,128)(2,1)S(1)} collective-permute-done((bf16[192,1536]{1,0:T(8,128)(2,1)S(1)}, bf16[192,1536]{1,0:T(8,128)(2,1)S(1)}, u32[]{:S(2)}, u32[]{:S(2)}) %collective-permute-start.8) | collective-permute-done | bytes 589856 | tf_op jit(solution)/shard_map/ppermute | solution.py:111
  77.0 2.4 collective-permute-start.10
  80.0 13.7 %collective-permute-done.10 = bf16[192,1536]{1,0:T(8,128)(2,1)S(1)} collective-permute-done((bf16[192,1536]{1,0:T(8,128)(2,1)S(1)}, bf16[192,1536]{1,0:T(8,128)(2,1)S(1)}, u32[]{:S(2)}, u32[]{:S(2)}) %collective-permute-start.10) | collective-permute-done | bytes 589856 | tf_op jit(solution)/shard_map/ppermute | solution.py:111
  93.8 4.8 %fusion.4 = (f32[1536]{0:T(1024)S(1)}, f32[1536]{0:T(1024)S(1)}, f32[192,1536]{1,0:T(8,128)}, f32[192,1536]{1,0:T(8,128)}) fusion(bf16[1,12,16,1536]{3,2,1,0:T(8,128)(2,1)S(1)} %copy-done.4, f32[1536]{0:T(1024)S(1)} %copy-done.44, bf16[192,1536]{1,0:T(8,128)(2,1)S(1)} %bitcast.106, bf16[1536,1536]{1,0:T(8,128)(2,1)S(1)} %bitcast.104), kind=kOutput, calls=%fused_computation.63 | convolution fusion | flops 926610432 | bytes 8275968 | tf_op jit(solution)/shard_map/dot_general | solution.py:272
  99.2 6.4 %all-reduce.2 = (f32[]{:T(128)}, f32[]{:T(128)}) all-reduce(f32[]{:T(128)} %get-tuple-element.117, f32[]{:T(128)} %get-tuple-element.116), channel_id=1, replica_groups=mesh['fsdp'=8,'rows'=4] {'rows'}, use_global_device_ids=true, to_apply=%region_4.5 | all-reduce | flops 2 | bytes 16 | tf_op jit(solution)/shard_map/psum | solution.py:277
  106.9 3.4 %fusion.3 = (bf16[192,1536]{1,0:T(8,128)(2,1)S(1)}, bf16[192,1536]{1,0:T(8,128)(2,1)}) fusion(f32[192,1536]{1,0:T(8,128)} %get-tuple-element.155, f32[192,1536]{1,0:T(8,128)} %get-tuple-element.124, bf16[1,12,16,1536]{3,2,1,0:T(8,128)(2,1)} %param.23, f32[1536]{0:T(1024)S(1)} %get-tuple-element.139, f32[1536]{0:T(1024)S(1)} %get-tuple-element.122, ...), kind=kLoop, calls=%fused_computation.62 | loop fusion | flops 5603328 | bytes 4159488 | tf_op jit(solution)/shard_map/convert_element_type | solution.py:284
  110.3 4.0 %convolution_convert_fusion.1 = bf16[12,16,1536]{2,1,0:T(8,128)(2,1)S(1)} fusion(bf16[12,16,1536]{2,1,0:T(8,128)(2,1)S(1)} %bitcast.108, bf16[1536,1536,1]{1,0,2:T(8,128)(2,1)} %bitcast.105), kind=kOutput, calls=%fused_computation.52 | convolution fusion | flops 906264576 | bytes 5898240 | tf_op jit(solution)/shard_map/hwf,cf->hwc/dot_general | solution.py:293
  131.9 1.7 collective-permute-start.12
  136.1 1.8 collective-permute-start.18
  138.1 3.3 %collective-permute-done.12 = f32[1,3,16,1536]{3,2,1,0:T(8,128)S(1)} collective-permute-done((f32[1,3,16,1536]{3,2,1,0:T(8,128)S(1)}, f32[1,3,16,1536]{3,2,1,0:T(8,128)S(1)}, u32[]{:S(2)}, u32[]{:S(2)}) %collective-permute-start.12) | collective-permute-done | bytes 294944 | tf_op jit(solution)/shard_map/ppermute | solution.py:68
  143.3 1.7 collective-permute-start.13
  148.8 2.6 collective-permute-start.22
  151.9 2.2 fusion.13
  154.2 1.8 collective-permute-start.19
  157.6 3.0 %collective-permute-done.23 = f32[1,18816]{1,0:T(1,128)S(1)} collective-permute-done((f32[1,18816]{1,0:T(1,128)S(1)}, f32[1,18816]{1,0:T(1,128)S(1)}, u32[]{:S(2)}, u32[]{:S(2)}) %collective-permute-start.23) | collective-permute-done | bytes 75296 | tf_op jit(solution)/shard_map/ppermute | solution.py:68
  161.4 3.7 %fusion.152 = bf16[1,3,16,1536]{3,2,1,0:T(8,128)(2,1)} fusion(f32[1536]{0:T(1024)} %copy-done.33, bf16[9,22,1536]{2,1,0:T(8,128)(2,1)S(1)} %select_maximum_fusion, f32[1536]{0:T(1024)} %copy-done.34, f32[1536]{0:T(1024)S(1)} %get-tuple-element.59, f32[1536]{0:T(1024)S(1)} %get-tuple-element.60, bf16[3,16,1536]{2,1,0:T(8,128)(2,1)S(1)} %collective-permute-done.13, ...), kind=kLoop, calls=%fused_computation.310 | loop fusion | flops 11132928 | bytes 7084032 | tf_op jit(solution)/shard_map/reshape | solution.py:312
  165.1 65.4 %all-reduce.5.cloned.1.call-done = f32[1,18816]{1,0:T(1,128)} async-done(((f32[1,18816]{1,0:T(1,128)}), f32[1,18816]{1,0:T(1,128)}) %all-reduce.5.cloned.1.call-update) | async-done | bytes 75280 | tf_op jit(solution)/shard_map/psum | solution.py:308
  230.5 1.6 fusion.15
  235.9 11.9 %collective-permute-done.16 = bf16[192,1536]{1,0:T(8,128)(2,1)S(1)} collective-permute-done((bf16[192,1536]{1,0:T(8,128)(2,1)S(1)}, bf16[192,1536]{1,0:T(8,128)(2,1)S(1)}, u32[]{:S(2)}, u32[]{:S(2)}) %collective-permute-start.16) | collective-permute-done | bytes 589856 | tf_op jit(solution)/shard_map/ppermute | solution.py:146
  250.4 1.7 collective-permute-start.17
  253.6 11.5 %collective-permute-done.17 = bf16[192,1536]{1,0:T(8,128)(2,1)S(1)} collective-permute-done((bf16[192,1536]{1,0:T(8,128)(2,1)S(1)}, bf16[192,1536]{1,0:T(8,128)(2,1)S(1)}, u32[]{:S(2)}, u32[]{:S(2)}) %collective-permute-start.17) | collective-permute-done | bytes 589856 | tf_op jit(solution)/shard_map/ppermute | solution.py:146
  266.4 2.3 fusion.16
  (219 shorter events, 34.5 us)
Async XLA Ops:
  7.2 223.3 %all-reduce.5.cloned.1.call-start = ((), (), s32[]{:S(2)}) async-start(), calls=%async_computation | async-start | bytes 150528 | tf_op jit(solution)/shard_map/psum | solution.py:308
  7.2 37.2 %collective-permute-start = (bf16[192,1536]{1,0:T(8,128)(2,1)}, bf16[192,1536]{1,0:T(8,128)(2,1)S(1)}, u32[]{:S(2)}, u32[]{:S(2)}) collective-permute-start(bf16[192,1536]{1,0:T(8,128)(2,1)} %param.19), channel_id=1, source_target_pairs={{0,8},{8,16},{16,24},{24,28},{28,20},{20,12},{12,4},{4,0},{1,9},{9... | collective-permute-start | bytes 1769480 | tf_op jit(solution)/shard_map/ppermute | solution.py:111
  10.3 34.2 %collective-permute-start.1 = (bf16[192,1536]{1,0:T(8,128)(2,1)}, bf16[192,1536]{1,0:T(8,128)(2,1)S(1)}, u32[]{:S(2)}, u32[]{:S(2)}) collective-permute-start(bf16[192,1536]{1,0:T(8,128)(2,1)} %param.19), channel_id=1, source_target_pairs={{0,4},{8,0},{16,8},{24,16},{28,24},{20,28},{12,20},{4,12},{1,5},{9... | collective-permute-start | bytes 1769480 | tf_op jit(solution)/shard_map/ppermute | solution.py:113
  37.2 15.0 %copy-start.8 = (f32[1536]{0:T(1024)}, f32[1536]{0:T(1024)S(1)}, u32[]{:S(2)}) copy-start(f32[1536]{0:T(1024)S(1)} %get-tuple-element.87) | copy-start | bytes 18436
  37.2 15.0 %copy-start.10 = (f32[1536]{0:T(1024)}, f32[1536]{0:T(1024)S(1)}, u32[]{:S(2)}) copy-start(f32[1536]{0:T(1024)S(1)} %get-tuple-element.88) | copy-start | bytes 18436
  37.3 15.0 %copy-start.12 = (f32[1536]{0:T(1024)}, f32[1536]{0:T(1024)S(1)}, u32[]{:S(2)}) copy-start(f32[1536]{0:T(1024)S(1)} %get-tuple-element.89) | copy-start | bytes 18436
  37.3 15.0 %copy-start.14 = (f32[1536]{0:T(1024)}, f32[1536]{0:T(1024)S(1)}, u32[]{:S(2)}) copy-start(f32[1536]{0:T(1024)S(1)} %get-tuple-element.90) | copy-start | bytes 18436
  37.3 15.0 %copy-start.16 = (f32[1536]{0:T(1024)}, f32[1536]{0:T(1024)S(1)}, u32[]{:S(2)}) copy-start(f32[1536]{0:T(1024)S(1)} %get-tuple-element.91) | copy-start | bytes 18436
  45.3 4.9 %collective-permute-start.2 = (bf16[3,16,1536]{2,1,0:T(8,128)(2,1)S(1)}, bf16[3,16,1536]{2,1,0:T(8,128)(2,1)S(1)}, u32[]{:S(2)}, u32[]{:S(2)}) collective-permute-start(bf16[3,16,1536]{2,1,0:T(8,128)(2,1)S(1)} %bitcast.109), channel_id=1, source_target_pairs={{0,1},{1,2},{2,3},{4,5},{5,6},{6,7},{8,9},{9,10},{10,11},{12,13},{... | collective-permute-start | bytes 442376 | tf_op jit(solution)/shard_map/ppermute | solution.py:15
  46.8 5.3 %collective-permute-start.3 = (bf16[3,16,1536]{2,1,0:T(8,128)(2,1)S(1)}, bf16[3,16,1536]{2,1,0:T(8,128)(2,1)S(1)}, u32[]{:S(2)}, u32[]{:S(2)}) collective-permute-start(bf16[3,16,1536]{2,1,0:T(8,128)(2,1)S(1)} %bitcast.110), channel_id=1, source_target_pairs={{1,0},{2,1},{3,2},{5,4},{6,5},{7,6},{9,8},{10,9},{11,10},{13,12},{... | collective-permute-start | bytes 442376 | tf_op jit(solution)/shard_map/ppermute | solution.py:18
  48.1 14.0 %collective-permute-start.6 = (bf16[192,1536]{1,0:T(8,128)(2,1)S(1)}, bf16[192,1536]{1,0:T(8,128)(2,1)S(1)}, u32[]{:S(2)}, u32[]{:S(2)}) collective-permute-start(bf16[192,1536]{1,0:T(8,128)(2,1)S(1)} %collective-permute-done), channel_id=1, source_target_pairs={{0,8},{8,16},{16,24},{24,28},{28,20},{20,12},{12,4},{4,0},{1,9},{9... | collective-permute-start | bytes 1769480 | tf_op jit(solution)/shard_map/ppermute | solution.py:111
  49.9 14.5 %collective-permute-start.7 = (bf16[192,1536]{1,0:T(8,128)(2,1)S(1)}, bf16[192,1536]{1,0:T(8,128)(2,1)S(1)}, u32[]{:S(2)}, u32[]{:S(2)}) collective-permute-start(bf16[192,1536]{1,0:T(8,128)(2,1)S(1)} %collective-permute-done.1), channel_id=1, source_target_pairs={{0,4},{8,0},{16,8},{24,16},{28,24},{20,28},{12,20},{4,12},{1,5},{9... | collective-permute-start | bytes 1769480 | tf_op jit(solution)/shard_map/ppermute | solution.py:113
  56.3 5.1 %collective-permute-start.4 = (bf16[1,3,16,1536]{3,2,1,0:T(8,128)(2,1)S(1)}, bf16[1,3,16,1536]{3,2,1,0:T(8,128)(2,1)S(1)}, u32[]{:S(2)}, u32[]{:S(2)}) collective-permute-start(bf16[1,3,16,1536]{3,2,1,0:T(8,128)(2,1)S(1)} %fusion.149), channel_id=1, source_target_pairs={{0,1},{1,0},{2,3},{3,2},{4,5},{5,4},{6,7},{7,6},{8,9},{9,8},{10,11... | collective-permute-start | bytes 442376 | tf_op jit(solution)/shard_map/ppermute | solution.py:169
  61.4 9.3 %collective-permute-start.5 = (bf16[2,3,16,1536]{3,2,1,0:T(8,128)(2,1)S(1)}, bf16[2,3,16,1536]{3,2,1,0:T(8,128)(2,1)S(1)}, u32[]{:S(2)}, u32[]{:S(2)}) collective-permute-start(bf16[2,3,16,1536]{3,2,1,0:T(8,128)(2,1)S(1)} %maximum_select_fusion.2), channel_id=1, source_target_pairs={{0,2},{1,3},{2,0},{3,1},{4,6},{5,7},{6,4},{7,5},{8,10},{9,11},{10,... | collective-permute-start | bytes 884744 | tf_op jit(solution)/shard_map/ppermute | solution.py:169
  62.1 14.9 %collective-permute-start.8 = (bf16[192,1536]{1,0:T(8,128)(2,1)S(1)}, bf16[192,1536]{1,0:T(8,128)(2,1)S(1)}, u32[]{:S(2)}, u32[]{:S(2)}) collective-permute-start(bf16[192,1536]{1,0:T(8,128)(2,1)S(1)} %collective-permute-done.6), channel_id=1, source_target_pairs={{0,8},{8,16},{16,24},{24,28},{28,20},{20,12},{12,4},{4,0},{1,9},{9... | collective-permute-start | bytes 1769480 | tf_op jit(solution)/shard_map/ppermute | solution.py:111
  64.5 15.4 %collective-permute-start.9 = (bf16[192,1536]{1,0:T(8,128)(2,1)S(1)}, bf16[192,1536]{1,0:T(8,128)(2,1)S(1)}, u32[]{:S(2)}, u32[]{:S(2)}) collective-permute-start(bf16[192,1536]{1,0:T(8,128)(2,1)S(1)} %collective-permute-done.7), channel_id=1, source_target_pairs={{0,4},{8,0},{16,8},{24,16},{28,24},{20,28},{12,20},{4,12},{1,5},{9... | collective-permute-start | bytes 1769480 | tf_op jit(solution)/shard_map/ppermute | solution.py:113
  77.0 16.7 %collective-permute-start.10 = (bf16[192,1536]{1,0:T(8,128)(2,1)S(1)}, bf16[192,1536]{1,0:T(8,128)(2,1)S(1)}, u32[]{:S(2)}, u32[]{:S(2)}) collective-permute-start(bf16[192,1536]{1,0:T(8,128)(2,1)S(1)} %collective-permute-done.8), channel_id=1, source_target_pairs={{0,8},{8,16},{16,24},{24,28},{28,20},{20,12},{12,4},{4,0},{1,9},{9... | collective-permute-start | bytes 1769480 | tf_op jit(solution)/shard_map/ppermute | solution.py:111
  115.9 14.8 %collective-permute-start.11 = (bf16[2,3,16,1536]{3,2,1,0:T(8,128)(2,1)}, bf16[2,3,16,1536]{3,2,1,0:T(8,128)(2,1)}, u32[]{:S(2)}, u32[]{:S(2)}) collective-permute-start(bf16[2,3,16,1536]{3,2,1,0:T(8,128)(2,1)} %dynamic-slice_bitcast_fusion.2), channel_id=1, source_target_pairs={{0,1},{1,0},{2,3},{3,2},{4,5},{5,4},{6,7},{7,6},{8,9},{9,8},{10,11... | collective-permute-start | bytes 884744 | tf_op jit(solution)/shard_map/ppermute | solution.py:68
  131.9 9.5 %collective-permute-start.12 = (f32[1,3,16,1536]{3,2,1,0:T(8,128)S(1)}, f32[1,3,16,1536]{3,2,1,0:T(8,128)S(1)}, u32[]{:S(2)}, u32[]{:S(2)}) collective-permute-start(f32[1,3,16,1536]{3,2,1,0:T(8,128)S(1)} %constant_dynamic-slice_fusion.3), channel_id=1, source_target_pairs={{0,2},{1,3},{2,0},{3,1},{4,6},{5,7},{6,4},{7,5},{8,10},{9,11},{10,... | collective-permute-start | bytes 884744 | tf_op jit(solution)/shard_map/ppermute | solution.py:68
  136.1 15.9 %collective-permute-start.18 = (bf16[192,1536]{1,0:T(8,128)(2,1)}, bf16[192,1536]{1,0:T(8,128)(2,1)}, u32[]{:S(2)}, u32[]{:S(2)}) collective-permute-start(bf16[192,1536]{1,0:T(8,128)(2,1)} %get-tuple-element.132), channel_id=1, source_target_pairs={{0,8},{8,16},{16,24},{24,28},{28,20},{20,12},{12,4},{4,0},{1,9},{9... | collective-permute-start | bytes 1769480 | tf_op jit(solution)/shard_map/ppermute | solution.py:144
  137.9 92.6 %collective-permute-start.15 = (bf16[192,1536]{1,0:T(8,128)(2,1)S(1)}, bf16[192,1536]{1,0:T(8,128)(2,1)S(1)}, u32[]{:S(2)}, u32[]{:S(2)}) collective-permute-start(bf16[192,1536]{1,0:T(8,128)(2,1)S(1)} %get-tuple-element.131), channel_id=1, source_target_pairs={{0,4},{8,0},{16,8},{24,16},{28,24},{20,28},{12,20},{4,12},{1,5},{9... | collective-permute-start | bytes 1769480 | tf_op jit(solution)/shard_map/ppermute | solution.py:146
  143.3 14.1 %collective-permute-start.13 = (bf16[3,16,1536]{2,1,0:T(8,128)(2,1)S(1)}, bf16[3,16,1536]{2,1,0:T(8,128)(2,1)S(1)}, u32[]{:S(2)}, u32[]{:S(2)}) collective-permute-start(bf16[3,16,1536]{2,1,0:T(8,128)(2,1)S(1)} %get-tuple-element.120), channel_id=1, source_target_pairs={{0,1},{1,2},{2,3},{4,5},{5,6},{6,7},{8,9},{9,10},{10,11},{12,13},{... | collective-permute-start | bytes 442376 | tf_op jit(solution)/shard_map/ppermute | solution.py:15
  145.0 12.3 %collective-permute-start.14 = (bf16[3,16,1536]{2,1,0:T(8,128)(2,1)S(1)}, bf16[3,16,1536]{2,1,0:T(8,128)(2,1)S(1)}, u32[]{:S(2)}, u32[]{:S(2)}) collective-permute-start(bf16[3,16,1536]{2,1,0:T(8,128)(2,1)S(1)} %get-tuple-element.120), channel_id=1, source_target_pairs={{1,0},{2,1},{3,2},{5,4},{6,5},{7,6},{9,8},{10,9},{11,10},{13,12},{... | collective-permute-start | bytes 442376 | tf_op jit(solution)/shard_map/ppermute | solution.py:18
  148.8 7.2 %collective-permute-start.22 = (f32[2,18816]{1,0:T(2,128)S(1)}, f32[2,18816]{1,0:T(2,128)S(1)}, u32[]{:S(2)}, u32[]{:S(2)}) collective-permute-start(f32[2,18816]{1,0:T(2,128)S(1)} %bitcast.118), channel_id=1, source_target_pairs={{0,1},{1,0},{2,3},{3,2},{4,5},{5,4},{6,7},{7,6},{8,9},{9,8},{10,11... | collective-permute-start | bytes 451592 | tf_op jit(solution)/shard_map/ppermute | solution.py:68
  154.2 76.3 %collective-permute-start.19 = (bf16[192,1536]{1,0:T(8,128)(2,1)}, bf16[192,1536]{1,0:T(8,128)(2,1)S(1)}, u32[]{:S(2)}, u32[]{:S(2)}) collective-permute-start(bf16[192,1536]{1,0:T(8,128)(2,1)} %fusion.13), channel_id=1, source_target_pairs={{0,8},{8,16},{16,24},{24,28},{28,20},{20,12},{12,4},{4,0},{1,9},{9... | collective-permute-start | bytes 1769480 | tf_op jit(solution)/shard_map/ppermute | solution.py:144
  156.1 4.4 %collective-permute-start.23 = (f32[1,18816]{1,0:T(1,128)S(1)}, f32[1,18816]{1,0:T(1,128)S(1)}, u32[]{:S(2)}, u32[]{:S(2)}) collective-permute-start(f32[1,18816]{1,0:T(1,128)S(1)} %constant_dynamic-slice_fusion), channel_id=1, source_target_pairs={{0,2},{1,3},{2,0},{3,1},{4,6},{5,7},{6,4},{7,5},{8,10},{9,11},{10,... | collective-permute-start | bytes 225800 | tf_op jit(solution)/shard_map/ppermute | solution.py:68
  230.4 3.7 %collective-permute-start.24 = (f32[1,18816]{1,0:T(1,128)}, f32[1,18816]{1,0:T(1,128)S(1)}, u32[]{:S(2)}, u32[]{:S(2)}) collective-permute-start(f32[1,18816]{1,0:T(1,128)} %all-reduce.5.cloned.1.call-done), channel_id=1, source_target_pairs={{0,1},{1,0},{2,3},{3,2},{4,5},{5,4},{6,7},{7,6},{8,9},{9,8},{10,11... | collective-permute-start | bytes 225800 | tf_op jit(solution)/shard_map/ppermute | solution.py:169
  232.0 15.8 %collective-permute-start.16 = (bf16[192,1536]{1,0:T(8,128)(2,1)S(1)}, bf16[192,1536]{1,0:T(8,128)(2,1)S(1)}, u32[]{:S(2)}, u32[]{:S(2)}) collective-permute-start(bf16[192,1536]{1,0:T(8,128)(2,1)S(1)} %get-tuple-element.129), channel_id=1, source_target_pairs={{0,4},{8,0},{16,8},{24,16},{28,24},{20,28},{12,20},{4,12},{1,5},{9... | collective-permute-start | bytes 1769480 | tf_op jit(solution)/shard_map/ppermute | solution.py:146
  233.5 15.4 %collective-permute-start.20 = (bf16[192,1536]{1,0:T(8,128)(2,1)S(1)}, bf16[192,1536]{1,0:T(8,128)(2,1)S(1)}, u32[]{:S(2)}, u32[]{:S(2)}) collective-permute-start(bf16[192,1536]{1,0:T(8,128)(2,1)S(1)} %get-tuple-element.130), channel_id=1, source_target_pairs={{0,8},{8,16},{16,24},{24,28},{28,20},{20,12},{12,4},{4,0},{1,9},{9... | collective-permute-start | bytes 1769480 | tf_op jit(solution)/shard_map/ppermute | solution.py:144
  234.4 18.1 %collective-permute-start.25 = (f32[2,18816]{1,0:T(2,128)S(1)}, f32[2,18816]{1,0:T(2,128)S(1)}, u32[]{:S(2)}, u32[]{:S(2)}) collective-permute-start(f32[2,18816]{1,0:T(2,128)S(1)} %maximum_select_fusion.3), channel_id=1, source_target_pairs={{0,2},{1,3},{2,0},{3,1},{4,6},{5,7},{6,4},{7,5},{8,10},{9,11},{10,... | collective-permute-start | bytes 451592 | tf_op jit(solution)/shard_map/ppermute | solution.py:169
  250.4 14.6 %collective-permute-start.17 = (bf16[192,1536]{1,0:T(8,128)(2,1)S(1)}, bf16[192,1536]{1,0:T(8,128)(2,1)S(1)}, u32[]{:S(2)}, u32[]{:S(2)}) collective-permute-start(bf16[192,1536]{1,0:T(8,128)(2,1)S(1)} %get-tuple-element.127), channel_id=1, source_target_pairs={{0,4},{8,0},{16,8},{24,16},{28,24},{20,28},{12,20},{4,12},{1,5},{9... | collective-permute-start | bytes 1769480 | tf_op jit(solution)/shard_map/ppermute | solution.py:146
  252.1 14.3 %collective-permute-start.21 = (bf16[192,1536]{1,0:T(8,128)(2,1)S(1)}, bf16[192,1536]{1,0:T(8,128)(2,1)S(1)}, u32[]{:S(2)}, u32[]{:S(2)}) collective-permute-start(bf16[192,1536]{1,0:T(8,128)(2,1)S(1)} %get-tuple-element.128), channel_id=1, source_target_pairs={{0,8},{8,16},{16,24},{24,28},{28,20},{20,12},{12,4},{4,0},{1,9},{9... | collective-permute-start | bytes 1769480 | tf_op jit(solution)/shard_map/ppermute | solution.py:144
  (40 other events, 315.9 us)
Sparse Core Ops, SparseCore 0:
  161.4 68.9 all-reduce.4
where the time goes:
time: 277 us; the launch traced here: 276 us
  waiting for transfers between devices  128 us (46%)
  between operations  56.1 us (20%)
  starting transfers between devices  34.7 us (13%)
  other arithmetic  24.5 us (9%)
  local copies, waits for them, and re-layouts  15.5 us (6%)
  matrix products  10.3 us (4%)
  blocking collectives  6.37 us (2%)
    psum x1, waiting for transfers between devices, body(): lax.psum(kernel_part, 'fsdp')  65.4 us
    ppermute x3, waiting for transfers between devices, ring_reduce_scatter(): ccw = lax.ppermute(ccw, axis, backward)  23.4 us
    ppermute x4, waiting for transfers between devices, ring_all_gather(): cw = lax.ppermute(cw, axis, forward)  20.5 us
    ppermute x4, starting transfers between devices, ring_all_gather(): cw = lax.ppermute(cw, axis, forward)  9.53 us
    ppermute x4, waiting for transfers between devices, tree_all_gather(): other = lax.ppermute(data, axis, perm)  7.08 us
    psum x1, blocking collectives, body(): norm_total = lax.psum(jnp.sum(norms), 'rows')  6.37 us
    ppermute x4, waiting for transfers between devices, tree_reduce_scatter(): lax.ppermute(give, axis, perm).astype(jnp.float32)  6.24 us
    ppermute x4, starting transfers between devices, tree_all_gather(): other = lax.ppermute(data, axis, perm)  5.65 us
  transfers between devices with their start and end apart: 27, of which 16 were waited for; matrix products, arithmetic and copies ran while one was open for 11% of the time, Pallas kernels for 0%

commit v1 on v0

--- a/solution.py
+++ b/solution.py
@@ -305,9 +305,12 @@
     kernel_local = kern_grad(padded, activation_gradient)
     n_rows = lax.axis_size("rows")
     kernel_part = tree_reduce_scatter(kernel_local.reshape(n_rows, -1), "rows")
-    kernel_total = tree_all_gather(lax.psum(kernel_part, "fsdp"), "rows").reshape(
-        kernel_local.shape
-    )
+
+    def _change_plate(sheet):
+        z1 = jnp.sum(lax.all_gather(sheet, "fsdp"), axis=0)
+        return z1
+
+    kernel_total = tree_all_gather(_change_plate(kernel_part), "rows").reshape(kernel_local.shape)
     activation = output.reshape(1, height, cols, -1)
     return (activation, dframe.reshape((1,) + dframe.shape), up_grad, kernel_total)
 

time: 277 us -> 229 us (0.83)
  waiting for transfers between devices: 128 us -> 57.3 us
  blocking collectives: 6.37 us -> 41.2 us
  between operations: 56.1 us -> 43.8 us
    psum x1 -> x0, waiting for transfers between devices: 65.4 us -> none  [body(): lax.psum(kernel_part, 'fsdp')]
    all_gather x0 -> x1, blocking collectives: none -> 34.8 us  [_change_plate(): z1 = jnp.sum(lax.all_gather(sheet, 'fsdp'), axis=0)]
    ppermute x4, waiting for transfers between devices: 6.24 us -> 3.26 us  [tree_reduce_scatter(): lax.ppermute(give, axis, perm).astype(jnp.float32)]
  transfers between devices with their start and end apart: 27 -> 26, of which waited for: 16 -> 14; matrix products, arithmetic and copies ran while one was open for 11% -> 13% of each run, Pallas kernels for 0% -> 0%
where the time goes in v1:
time: 229 us; the launch traced here: 228 us
  waiting for transfers between devices  57.3 us (25%)
  between operations  43.8 us (19%)
  blocking collectives  41.2 us (18%)
  starting transfers between devices  35.5 us (16%)
  other arithmetic  24.3 us (11%)
  local copies, waits for them, and re-layouts  15.1 us (7%)
  matrix products  10.3 us (4%)
    all_gather x1, blocking collectives, _change_plate(): z1 = jnp.sum(lax.all_gather(sheet, 'fsdp'), axis=0)  34.8 us
    ppermute x3, waiting for transfers between devices, ring_reduce_scatter(): ccw = lax.ppermute(ccw, axis, backward)  22.9 us
    ppermute x4, waiting for transfers between devices, ring_all_gather(): cw = lax.ppermute(cw, axis, forward)  20.2 us
    ppermute x4, starting transfers between devices, ring_all_gather(): cw = lax.ppermute(cw, axis, forward)  9.53 us
    ppermute x4, waiting for transfers between devices, tree_all_gather(): other = lax.ppermute(data, axis, perm)  7.24 us
    ppermute x4, starting transfers between devices, ring_reduce_scatter(): cw = lax.ppermute(cw, axis, forward)  7.1 us
    ppermute x4, starting transfers between devices, tree_all_gather(): other = lax.ppermute(data, axis, perm)  6.46 us
    psum x1, blocking collectives, body(): norm_total = lax.psum(jnp.sum(norms), 'rows')  6.43 us
  transfers between devices with their start and end apart: 26, of which 14 were waited for; matrix products, arithmetic and copies ran while one was open for 13% of the time, Pallas kernels for 0%

profile of v1, /device:TPU:0, one launch (start us, length us, event | category | flops | bytes accessed | tf_op | source)
XLA Modules:
  0.0 227.5 jit_solution(4696500118050670771)
XLA Ops:
  0.6 3.1 %collective-permute-start = (bf16[192,1536]{1,0:T(8,128)(2,1)}, bf16[192,1536]{1,0:T(8,128)(2,1)S(1)}, u32[]{:S(2)}, u32[]{:S(2)}) collective-permute-start(bf16[192,1536]{1,0:T(8,128)(2,1)} %param.19), channel_id=1, source_target_pairs={{0,8},{8,16},{16,24},{24,28},{28,20},{20,12},{12,4},{4,0},{1,9},{9... | collective-permute-start | bytes 1769480 | tf_op jit(solution)/shard_map/ppermute | solution.py:111
  16.2 2.0 fusion.160
  27.2 1.7 slice_reduce_fusion.48
  29.0 1.8 slice_reduce_fusion.47
  41.7 1.9 collective-permute-start.6
  43.9 1.8 collective-permute-done.3
  46.3 3.4 %fusion.158 = (f32[3,16]{1,0:T(4,128)S(1)}, f32[3,16,1536]{2,1,0:T(8,128)S(1)}) fusion(f32[1536]{0:T(1024)S(1)} %get-tuple-element.105, bf16[9,22,1536]{2,1,0:T(8,128)(2,1)S(1)} %select_maximum_fusion.2, f32[1536]{0:T(1024)S(1)} %get-tuple-element.106, f32[1536]{0:T(1024)S(1)} %get-tuple-element.59, f32[1536]{0:T(1024)S(1)} %get-tuple-element.60, ...), kind=kLoop, calls=%fused_computation.380 | loop fusion | flops 10911696 | bytes 7827648 | tf_op jit(solution)/shard_map/reduce_sum | solution.py:215
  50.1 4.1 %collective-permute-start.4 = (bf16[1,3,16,1536]{3,2,1,0:T(8,128)(2,1)S(1)}, bf16[1,3,16,1536]{3,2,1,0:T(8,128)(2,1)S(1)}, u32[]{:S(2)}, u32[]{:S(2)}) collective-permute-start(bf16[1,3,16,1536]{3,2,1,0:T(8,128)(2,1)S(1)} %fusion.149), channel_id=1, source_target_pairs={{0,1},{1,0},{2,3},{3,2},{4,5},{5,4},{6,7},{7,6},{8,9},{9,8},{10,11... | collective-permute-start | bytes 442376 | tf_op jit(solution)/shard_map/ppermute | solution.py:169
  55.8 2.1 collective-permute-start.8
  58.3 6.3 %collective-permute-done.5 = bf16[2,3,16,1536]{3,2,1,0:T(8,128)(2,1)S(1)} collective-permute-done((bf16[2,3,16,1536]{3,2,1,0:T(8,128)(2,1)S(1)}, bf16[2,3,16,1536]{3,2,1,0:T(8,128)(2,1)S(1)}, u32[]{:S(2)}, u32[]{:S(2)}) %collective-permute-start.5) | collective-permute-done | bytes 294944 | tf_op jit(solution)/shard_map/ppermute | solution.py:169
  64.7 6.0 %collective-permute-done.8 = bf16[192,1536]{1,0:T(8,128)(2,1)S(1)} collective-permute-done((bf16[192,1536]{1,0:T(8,128)(2,1)S(1)}, bf16[192,1536]{1,0:T(8,128)(2,1)S(1)}, u32[]{:S(2)}, u32[]{:S(2)}) %collective-permute-start.8) | collective-permute-done | bytes 589856 | tf_op jit(solution)/shard_map/ppermute | solution.py:111
  70.7 2.4 %collective-permute-start.10 = (bf16[192,1536]{1,0:T(8,128)(2,1)S(1)}, bf16[192,1536]{1,0:T(8,128)(2,1)S(1)}, u32[]{:S(2)}, u32[]{:S(2)}) collective-permute-start(bf16[192,1536]{1,0:T(8,128)(2,1)S(1)} %collective-permute-done.8), channel_id=1, source_target_pairs={{0,8},{8,16},{16,24},{24,28},{28,20},{20,12},{12,4},{4,0},{1,9},{9... | collective-permute-start | bytes 1769480 | tf_op jit(solution)/shard_map/ppermute | solution.py:111
  73.6 13.7 %collective-permute-done.10 = bf16[192,1536]{1,0:T(8,128)(2,1)S(1)} collective-permute-done((bf16[192,1536]{1,0:T(8,128)(2,1)S(1)}, bf16[192,1536]{1,0:T(8,128)(2,1)S(1)}, u32[]{:S(2)}, u32[]{:S(2)}) %collective-permute-start.10) | collective-permute-done | bytes 589856 | tf_op jit(solution)/shard_map/ppermute | solution.py:111
  87.5 4.8 %fusion.4 = (f32[1536]{0:T(1024)S(1)}, f32[1536]{0:T(1024)S(1)}, f32[192,1536]{1,0:T(8,128)}, f32[192,1536]{1,0:T(8,128)}) fusion(bf16[1,12,16,1536]{3,2,1,0:T(8,128)(2,1)S(1)} %copy-done.4, f32[1536]{0:T(1024)S(1)} %copy-done.92, bf16[192,1536]{1,0:T(8,128)(2,1)S(1)} %bitcast.108, bf16[1536,1536]{1,0:T(8,128)(2,1)S(1)} %bitcast.106), kind=kOutput, calls=%fused_computation.63 | convolution fusion | flops 926610432 | bytes 8275968 | tf_op jit(solution)/shard_map/dot_general | solution.py:272
  92.9 6.4 %all-reduce.2 = (f32[]{:T(128)}, f32[]{:T(128)}) all-reduce(f32[]{:T(128)} %get-tuple-element.117, f32[]{:T(128)} %get-tuple-element.116), channel_id=1, replica_groups=mesh['fsdp'=8,'rows'=4] {'rows'}, use_global_device_ids=true, to_apply=%region_4.5 | all-reduce | flops 2 | bytes 16 | tf_op jit(solution)/shard_map/psum | solution.py:277
  100.7 3.4 %fusion.3 = (bf16[192,1536]{1,0:T(8,128)(2,1)S(1)}, bf16[192,1536]{1,0:T(8,128)(2,1)}) fusion(f32[192,1536]{1,0:T(8,128)} %get-tuple-element.155, f32[192,1536]{1,0:T(8,128)} %get-tuple-element.124, bf16[1,12,16,1536]{3,2,1,0:T(8,128)(2,1)} %param.23, f32[1536]{0:T(1024)S(1)} %get-tuple-element.139, f32[1536]{0:T(1024)S(1)} %get-tuple-element.122, ...), kind=kLoop, calls=%fused_computation.62 | loop fusion | flops 5603328 | bytes 4159488 | tf_op jit(solution)/shard_map/convert_element_type | solution.py:284
  104.1 4.0 %convolution_convert_fusion.1 = bf16[12,16,1536]{2,1,0:T(8,128)(2,1)S(1)} fusion(bf16[12,16,1536]{2,1,0:T(8,128)(2,1)S(1)} %bitcast.110, bf16[1536,1536,1]{1,0,2:T(8,128)(2,1)} %bitcast.107), kind=kOutput, calls=%fused_computation.52 | convolution fusion | flops 906264576 | bytes 5898240 | tf_op jit(solution)/shard_map/hwf,cf->hwc/dot_general | solution.py:293
  125.2 1.7 collective-permute-start.12
  129.3 1.8 collective-permute-start.18
  131.4 3.3 %collective-permute-done.12 = f32[1,3,16,1536]{3,2,1,0:T(8,128)S(1)} collective-permute-done((f32[1,3,16,1536]{3,2,1,0:T(8,128)S(1)}, f32[1,3,16,1536]{3,2,1,0:T(8,128)S(1)}, u32[]{:S(2)}, u32[]{:S(2)}) %collective-permute-start.12) | collective-permute-done | bytes 294944 | tf_op jit(solution)/shard_map/ppermute | solution.py:68
  136.6 1.7 collective-permute-start.13
  142.0 2.6 %collective-permute-start.22 = (f32[2,18816]{1,0:T(2,128)S(1)}, f32[2,18816]{1,0:T(2,128)S(1)}, u32[]{:S(2)}, u32[]{:S(2)}) collective-permute-start(f32[2,18816]{1,0:T(2,128)S(1)} %bitcast.120), channel_id=1, source_target_pairs={{0,1},{1,0},{2,3},{3,2},{4,5},{5,4},{6,7},{7,6},{8,9},{9,8},{10,11... | collective-permute-start | bytes 451592 | tf_op jit(solution)/shard_map/ppermute | solution.py:68
  147.0 1.7 collective-permute-start.19
  151.7 3.7 %fusion.152 = bf16[1,3,16,1536]{3,2,1,0:T(8,128)(2,1)} fusion(f32[1536]{0:T(1024)S(1)} %copy-done.80, bf16[9,22,1536]{2,1,0:T(8,128)(2,1)S(1)} %select_maximum_fusion, f32[1536]{0:T(1024)S(1)} %copy-done.82, f32[1536]{0:T(1024)S(1)} %get-tuple-element.59, f32[1536]{0:T(1024)S(1)} %get-tuple-element.60, bf16[3,16,1536]{2,1,0:T(8,128)(2,1)S(1)} %collective-permute-done.13, ...), kind=kLoop, calls=%fused_computation.310 | loop fusion | flops 11132928 | bytes 7084032 | tf_op jit(solution)/shard_map/reshape | solution.py:315
  155.4 34.8 %all-gather = f32[8,1,18816]{2,1,0:T(1,128)S(1)} all-gather(f32[1,1,18816]{2,1,0:T(1,128)S(1)} %add_bitcast_fusion), channel_id=1, replica_groups=mesh['fsdp'=8,'rows'=4] {'fsdp'}, dimensions={0}, use_global_device_ids=true | all-gather | bytes 677376 | tf_op jit(solution)/shard_map/all_gather | solution.py:310
  190.8 1.6 fusion.15
  192.7 1.8 collective-permute-start.20
  194.7 2.3 collective-permute-start.25
  196.9 11.2 %collective-permute-done.16 = bf16[192,1536]{1,0:T(8,128)(2,1)S(1)} collective-permute-done((bf16[192,1536]{1,0:T(8,128)(2,1)S(1)}, bf16[192,1536]{1,0:T(8,128)(2,1)S(1)}, u32[]{:S(2)}, u32[]{:S(2)}) %collective-permute-start.16) | collective-permute-done | bytes 589856 | tf_op jit(solution)/shard_map/ppermute | solution.py:146
  210.0 1.8 collective-permute-start.21
  212.9 11.7 %collective-permute-done.17 = bf16[192,1536]{1,0:T(8,128)(2,1)S(1)} collective-permute-done((bf16[192,1536]{1,0:T(8,128)(2,1)S(1)}, bf16[192,1536]{1,0:T(8,128)(2,1)S(1)}, u32[]{:S(2)}, u32[]{:S(2)}) %collective-permute-start.17) | collective-permute-done | bytes 589856 | tf_op jit(solution)/shard_map/ppermute | solution.py:146
  225.2 2.3 %fusion.16 = f32[192,1536]{1,0:T(8,128)} fusion(bf16[192,1536]{1,0:T(8,128)(2,1)S(1)} %collective-permute-done.21, bf16[192,1536]{1,0:T(8,128)(2,1)S(1)} %collective-permute-done.17, bf16[8,192,1536]{2,1,0:T(8,128)(2,1)} %bitcast.105, s32[]{:T(128)S(6)} %select_n.294), kind=kLoop, calls=%fused_computation.81 | loop fusion | flops 1474560 | bytes 2949124 | tf_op jit(solution)/shard_map/add | solution.py:150
  (315 shorter events, 30.9 us)
Async XLA Ops:
  0.6 37.5 %collective-permute-start = (bf16[192,1536]{1,0:T(8,128)(2,1)}, bf16[192,1536]{1,0:T(8,128)(2,1)S(1)}, u32[]{:S(2)}, u32[]{:S(2)}) collective-permute-start(bf16[192,1536]{1,0:T(8,128)(2,1)} %param.19), channel_id=1, source_target_pairs={{0,8},{8,16},{16,24},{24,28},{28,20},{20,12},{12,4},{4,0},{1,9},{9... | collective-permute-start | bytes 1769480 | tf_op jit(solution)/shard_map/ppermute | solution.py:111
  3.7 34.4 %collective-permute-start.1 = (bf16[192,1536]{1,0:T(8,128)(2,1)}, bf16[192,1536]{1,0:T(8,128)(2,1)S(1)}, u32[]{:S(2)}, u32[]{:S(2)}) collective-permute-start(bf16[192,1536]{1,0:T(8,128)(2,1)} %param.19), channel_id=1, source_target_pairs={{0,4},{8,0},{16,8},{24,16},{28,24},{20,28},{12,20},{4,12},{1,5},{9... | collective-permute-start | bytes 1769480 | tf_op jit(solution)/shard_map/ppermute | solution.py:113
  28.9 17.0 %copy-start.7 = (f32[1536]{0:T(1024)}, f32[1536]{0:T(1024)S(1)}, u32[]{:S(2)}) copy-start(f32[1536]{0:T(1024)S(1)} %get-tuple-element.69) | copy-start | bytes 18436
  28.9 17.0 %copy-start.9 = (f32[1536]{0:T(1024)}, f32[1536]{0:T(1024)S(1)}, u32[]{:S(2)}) copy-start(f32[1536]{0:T(1024)S(1)} %get-tuple-element.70) | copy-start | bytes 18436
  28.9 17.0 %copy-start.11 = (f32[1536]{0:T(1024)}, f32[1536]{0:T(1024)S(1)}, u32[]{:S(2)}) copy-start(f32[1536]{0:T(1024)S(1)} %get-tuple-element.71) | copy-start | bytes 18436
  28.9 17.0 %copy-start.13 = (f32[1536]{0:T(1024)}, f32[1536]{0:T(1024)S(1)}, u32[]{:S(2)}) copy-start(f32[1536]{0:T(1024)S(1)} %get-tuple-element.72) | copy-start | bytes 18436
  29.0 17.0 %copy-start.15 = (f32[1536]{0:T(1024)}, f32[1536]{0:T(1024)S(1)}, u32[]{:S(2)}) copy-start(f32[1536]{0:T(1024)S(1)} %get-tuple-element.73) | copy-start | bytes 18436
  29.0 17.0 %copy-start.17 = (f32[1536]{0:T(1024)}, f32[1536]{0:T(1024)S(1)}, u32[]{:S(2)}) copy-start(f32[1536]{0:T(1024)S(1)} %get-tuple-element.74) | copy-start | bytes 18436
  39.0 4.9 %collective-permute-start.2 = (bf16[3,16,1536]{2,1,0:T(8,128)(2,1)S(1)}, bf16[3,16,1536]{2,1,0:T(8,128)(2,1)S(1)}, u32[]{:S(2)}, u32[]{:S(2)}) collective-permute-start(bf16[3,16,1536]{2,1,0:T(8,128)(2,1)S(1)} %bitcast.111), channel_id=1, source_target_pairs={{0,1},{1,2},{2,3},{4,5},{5,6},{6,7},{8,9},{9,10},{10,11},{12,13},{... | collective-permute-start | bytes 442376 | tf_op jit(solution)/shard_map/ppermute | solution.py:15
  40.4 5.3 %collective-permute-start.3 = (bf16[3,16,1536]{2,1,0:T(8,128)(2,1)S(1)}, bf16[3,16,1536]{2,1,0:T(8,128)(2,1)S(1)}, u32[]{:S(2)}, u32[]{:S(2)}) collective-permute-start(bf16[3,16,1536]{2,1,0:T(8,128)(2,1)S(1)} %bitcast.112), channel_id=1, source_target_pairs={{1,0},{2,1},{3,2},{5,4},{6,5},{7,6},{9,8},{10,9},{11,10},{13,12},{... | collective-permute-start | bytes 442376 | tf_op jit(solution)/shard_map/ppermute | solution.py:18
  41.7 14.0 %collective-permute-start.6 = (bf16[192,1536]{1,0:T(8,128)(2,1)S(1)}, bf16[192,1536]{1,0:T(8,128)(2,1)S(1)}, u32[]{:S(2)}, u32[]{:S(2)}) collective-permute-start(bf16[192,1536]{1,0:T(8,128)(2,1)S(1)} %collective-permute-done), channel_id=1, source_target_pairs={{0,8},{8,16},{16,24},{24,28},{28,20},{20,12},{12,4},{4,0},{1,9},{9... | collective-permute-start | bytes 1769480 | tf_op jit(solution)/shard_map/ppermute | solution.py:111
  43.6 14.5 %collective-permute-start.7 = (bf16[192,1536]{1,0:T(8,128)(2,1)S(1)}, bf16[192,1536]{1,0:T(8,128)(2,1)S(1)}, u32[]{:S(2)}, u32[]{:S(2)}) collective-permute-start(bf16[192,1536]{1,0:T(8,128)(2,1)S(1)} %collective-permute-done.1), channel_id=1, source_target_pairs={{0,4},{8,0},{16,8},{24,16},{28,24},{20,28},{12,20},{4,12},{1,5},{9... | collective-permute-start | bytes 1769480 | tf_op jit(solution)/shard_map/ppermute | solution.py:113
  50.1 5.1 %collective-permute-start.4 = (bf16[1,3,16,1536]{3,2,1,0:T(8,128)(2,1)S(1)}, bf16[1,3,16,1536]{3,2,1,0:T(8,128)(2,1)S(1)}, u32[]{:S(2)}, u32[]{:S(2)}) collective-permute-start(bf16[1,3,16,1536]{3,2,1,0:T(8,128)(2,1)S(1)} %fusion.149), channel_id=1, source_target_pairs={{0,1},{1,0},{2,3},{3,2},{4,5},{5,4},{6,7},{7,6},{8,9},{9,8},{10,11... | collective-permute-start | bytes 442376 | tf_op jit(solution)/shard_map/ppermute | solution.py:169
  55.2 9.3 %collective-permute-start.5 = (bf16[2,3,16,1536]{3,2,1,0:T(8,128)(2,1)S(1)}, bf16[2,3,16,1536]{3,2,1,0:T(8,128)(2,1)S(1)}, u32[]{:S(2)}, u32[]{:S(2)}) collective-permute-start(bf16[2,3,16,1536]{3,2,1,0:T(8,128)(2,1)S(1)} %maximum_select_fusion.2), channel_id=1, source_target_pairs={{0,2},{1,3},{2,0},{3,1},{4,6},{5,7},{6,4},{7,5},{8,10},{9,11},{10,... | collective-permute-start | bytes 884744 | tf_op jit(solution)/shard_map/ppermute | solution.py:169
  55.8 14.9 %collective-permute-start.8 = (bf16[192,1536]{1,0:T(8,128)(2,1)S(1)}, bf16[192,1536]{1,0:T(8,128)(2,1)S(1)}, u32[]{:S(2)}, u32[]{:S(2)}) collective-permute-start(bf16[192,1536]{1,0:T(8,128)(2,1)S(1)} %collective-permute-done.6), channel_id=1, source_target_pairs={{0,8},{8,16},{16,24},{24,28},{28,20},{20,12},{12,4},{4,0},{1,9},{9... | collective-permute-start | bytes 1769480 | tf_op jit(solution)/shard_map/ppermute | solution.py:111
  58.2 15.4 %collective-permute-start.9 = (bf16[192,1536]{1,0:T(8,128)(2,1)S(1)}, bf16[192,1536]{1,0:T(8,128)(2,1)S(1)}, u32[]{:S(2)}, u32[]{:S(2)}) collective-permute-start(bf16[192,1536]{1,0:T(8,128)(2,1)S(1)} %collective-permute-done.7), channel_id=1, source_target_pairs={{0,4},{8,0},{16,8},{24,16},{28,24},{20,28},{12,20},{4,12},{1,5},{9... | collective-permute-start | bytes 1769480 | tf_op jit(solution)/shard_map/ppermute | solution.py:113
  70.7 16.7 %collective-permute-start.10 = (bf16[192,1536]{1,0:T(8,128)(2,1)S(1)}, bf16[192,1536]{1,0:T(8,128)(2,1)S(1)}, u32[]{:S(2)}, u32[]{:S(2)}) collective-permute-start(bf16[192,1536]{1,0:T(8,128)(2,1)S(1)} %collective-permute-done.8), channel_id=1, source_target_pairs={{0,8},{8,16},{16,24},{24,28},{28,20},{20,12},{12,4},{4,0},{1,9},{9... | collective-permute-start | bytes 1769480 | tf_op jit(solution)/shard_map/ppermute | solution.py:111
  109.0 15.0 %collective-permute-start.11 = (bf16[2,3,16,1536]{3,2,1,0:T(8,128)(2,1)S(1)}, bf16[2,3,16,1536]{3,2,1,0:T(8,128)(2,1)}, u32[]{:S(2)}, u32[]{:S(2)}) collective-permute-start(bf16[2,3,16,1536]{3,2,1,0:T(8,128)(2,1)S(1)} %dynamic-slice_bitcast_fusion.2), channel_id=1, source_target_pairs={{0,1},{1,0},{2,3},{3,2},{4,5},{5,4},{6,7},{7,6},{8,9},{9,8},{10,11... | collective-permute-start | bytes 884744 | tf_op jit(solution)/shard_map/ppermute | solution.py:68
  125.2 9.5 %collective-permute-start.12 = (f32[1,3,16,1536]{3,2,1,0:T(8,128)S(1)}, f32[1,3,16,1536]{3,2,1,0:T(8,128)S(1)}, u32[]{:S(2)}, u32[]{:S(2)}) collective-permute-start(f32[1,3,16,1536]{3,2,1,0:T(8,128)S(1)} %constant_dynamic-slice_fusion.3), channel_id=1, source_target_pairs={{0,2},{1,3},{2,0},{3,1},{4,6},{5,7},{6,4},{7,5},{8,10},{9,11},{10,... | collective-permute-start | bytes 884744 | tf_op jit(solution)/shard_map/ppermute | solution.py:68
  129.3 15.9 %collective-permute-start.18 = (bf16[192,1536]{1,0:T(8,128)(2,1)}, bf16[192,1536]{1,0:T(8,128)(2,1)}, u32[]{:S(2)}, u32[]{:S(2)}) collective-permute-start(bf16[192,1536]{1,0:T(8,128)(2,1)} %get-tuple-element.132), channel_id=1, source_target_pairs={{0,8},{8,16},{16,24},{24,28},{28,20},{20,12},{12,4},{4,0},{1,9},{9... | collective-permute-start | bytes 1769480 | tf_op jit(solution)/shard_map/ppermute | solution.py:144
  131.1 59.7 %collective-permute-start.15 = (bf16[192,1536]{1,0:T(8,128)(2,1)S(1)}, bf16[192,1536]{1,0:T(8,128)(2,1)S(1)}, u32[]{:S(2)}, u32[]{:S(2)}) collective-permute-start(bf16[192,1536]{1,0:T(8,128)(2,1)S(1)} %get-tuple-element.131), channel_id=1, source_target_pairs={{0,4},{8,0},{16,8},{24,16},{28,24},{20,28},{12,20},{4,12},{1,5},{9... | collective-permute-start | bytes 1769480 | tf_op jit(solution)/shard_map/ppermute | solution.py:146
  136.6 12.2 %collective-permute-start.13 = (bf16[3,16,1536]{2,1,0:T(8,128)(2,1)S(1)}, bf16[3,16,1536]{2,1,0:T(8,128)(2,1)S(1)}, u32[]{:S(2)}, u32[]{:S(2)}) collective-permute-start(bf16[3,16,1536]{2,1,0:T(8,128)(2,1)S(1)} %get-tuple-element.120), channel_id=1, source_target_pairs={{0,1},{1,2},{2,3},{4,5},{5,6},{6,7},{8,9},{9,10},{10,11},{12,13},{... | collective-permute-start | bytes 442376 | tf_op jit(solution)/shard_map/ppermute | solution.py:15
  138.3 10.4 %collective-permute-start.14 = (bf16[3,16,1536]{2,1,0:T(8,128)(2,1)S(1)}, bf16[3,16,1536]{2,1,0:T(8,128)(2,1)}, u32[]{:S(2)}, u32[]{:S(2)}) collective-permute-start(bf16[3,16,1536]{2,1,0:T(8,128)(2,1)S(1)} %get-tuple-element.120), channel_id=1, source_target_pairs={{1,0},{2,1},{3,2},{5,4},{6,5},{7,6},{9,8},{10,9},{11,10},{13,12},{... | collective-permute-start | bytes 442376 | tf_op jit(solution)/shard_map/ppermute | solution.py:18
  142.0 7.9 %collective-permute-start.22 = (f32[2,18816]{1,0:T(2,128)S(1)}, f32[2,18816]{1,0:T(2,128)S(1)}, u32[]{:S(2)}, u32[]{:S(2)}) collective-permute-start(f32[2,18816]{1,0:T(2,128)S(1)} %bitcast.120), channel_id=1, source_target_pairs={{0,1},{1,0},{2,3},{3,2},{4,5},{5,4},{6,7},{7,6},{8,9},{9,8},{10,11... | collective-permute-start | bytes 451592 | tf_op jit(solution)/shard_map/ppermute | solution.py:68
  147.0 43.8 %collective-permute-start.19 = (bf16[192,1536]{1,0:T(8,128)(2,1)S(1)}, bf16[192,1536]{1,0:T(8,128)(2,1)S(1)}, u32[]{:S(2)}, u32[]{:S(2)}) collective-permute-start(bf16[192,1536]{1,0:T(8,128)(2,1)S(1)} %fusion.13), channel_id=1, source_target_pairs={{0,8},{8,16},{16,24},{24,28},{28,20},{20,12},{12,4},{4,0},{1,9},{9... | collective-permute-start | bytes 1769480 | tf_op jit(solution)/shard_map/ppermute | solution.py:144
  150.1 5.3 %collective-permute-start.23 = (f32[1,18816]{1,0:T(1,128)S(1)}, f32[1,18816]{1,0:T(1,128)S(1)}, u32[]{:S(2)}, u32[]{:S(2)}) collective-permute-start(f32[1,18816]{1,0:T(1,128)S(1)} %constant_dynamic-slice_fusion), channel_id=1, source_target_pairs={{0,2},{1,3},{2,0},{3,1},{4,6},{5,7},{6,4},{7,5},{8,10},{9,11},{10,... | collective-permute-start | bytes 225800 | tf_op jit(solution)/shard_map/ppermute | solution.py:68
  190.7 3.7 %collective-permute-start.24 = (f32[1,18816]{1,0:T(1,128)S(1)}, f32[1,18816]{1,0:T(1,128)S(1)}, u32[]{:S(2)}, u32[]{:S(2)}) collective-permute-start(f32[1,18816]{1,0:T(1,128)S(1)} %broadcast_in_dim.58), channel_id=1, source_target_pairs={{0,1},{1,0},{2,3},{3,2},{4,5},{5,4},{6,7},{7,6},{8,9},{9,8},{10,11... | collective-permute-start | bytes 225800 | tf_op jit(solution)/shard_map/ppermute | solution.py:169
  192.4 15.8 %collective-permute-start.16 = (bf16[192,1536]{1,0:T(8,128)(2,1)S(1)}, bf16[192,1536]{1,0:T(8,128)(2,1)S(1)}, u32[]{:S(2)}, u32[]{:S(2)}) collective-permute-start(bf16[192,1536]{1,0:T(8,128)(2,1)S(1)} %get-tuple-element.129), channel_id=1, source_target_pairs={{0,4},{8,0},{16,8},{24,16},{28,24},{20,28},{12,20},{4,12},{1,5},{9... | collective-permute-start | bytes 1769480 | tf_op jit(solution)/shard_map/ppermute | solution.py:146
  192.7 15.5 %collective-permute-start.20 = (bf16[192,1536]{1,0:T(8,128)(2,1)S(1)}, bf16[192,1536]{1,0:T(8,128)(2,1)S(1)}, u32[]{:S(2)}, u32[]{:S(2)}) collective-permute-start(bf16[192,1536]{1,0:T(8,128)(2,1)S(1)} %get-tuple-element.130), channel_id=1, source_target_pairs={{0,8},{8,16},{16,24},{24,28},{28,20},{20,12},{12,4},{4,0},{1,9},{9... | collective-permute-start | bytes 1769480 | tf_op jit(solution)/shard_map/ppermute | solution.py:144
  194.7 17.1 %collective-permute-start.25 = (f32[2,18816]{1,0:T(2,128)S(1)}, f32[2,18816]{1,0:T(2,128)S(1)}, u32[]{:S(2)}, u32[]{:S(2)}) collective-permute-start(f32[2,18816]{1,0:T(2,128)S(1)} %maximum_select_fusion.3), channel_id=1, source_target_pairs={{0,2},{1,3},{2,0},{3,1},{4,6},{5,7},{6,4},{7,5},{8,10},{9,11},{10,... | collective-permute-start | bytes 451592 | tf_op jit(solution)/shard_map/ppermute | solution.py:169
  209.7 14.9 %collective-permute-start.17 = (bf16[192,1536]{1,0:T(8,128)(2,1)S(1)}, bf16[192,1536]{1,0:T(8,128)(2,1)S(1)}, u32[]{:S(2)}, u32[]{:S(2)}) collective-permute-start(bf16[192,1536]{1,0:T(8,128)(2,1)S(1)} %get-tuple-element.127), channel_id=1, source_target_pairs={{0,4},{8,0},{16,8},{24,16},{28,24},{20,28},{12,20},{4,12},{1,5},{9... | collective-permute-start | bytes 1769480 | tf_op jit(solution)/shard_map/ppermute | solution.py:146
  210.0 15.2 %collective-permute-start.21 = (bf16[192,1536]{1,0:T(8,128)(2,1)S(1)}, bf16[192,1536]{1,0:T(8,128)(2,1)S(1)}, u32[]{:S(2)}, u32[]{:S(2)}) collective-permute-start(bf16[192,1536]{1,0:T(8,128)(2,1)S(1)} %get-tuple-element.128), channel_id=1, source_target_pairs={{0,8},{8,16},{16,24},{24,28},{28,20},{20,12},{12,4},{4,0},{1,9},{9... | collective-permute-start | bytes 1769480 | tf_op jit(solution)/shard_map/ppermute | solution.py:144
  (87 other events, 708.1 us)
